TPU v7x, 512 devices: a whole 4x4x16 slice. The times are simulated.
512 devices in a mesh: dp: 32 (over y, x, core), tensor: 16 (over z).
Axes of the slice: x: 4, y: 4, z: 16, core: 2. Of those that a mesh axis runs over, the one named last changes fastest.
Arguments:
- activations: bfloat16 [32768, 4096], P('dp', 'tensor'), may hold values from -40 to 40
- labels: int32 [32768], P('dp'), may hold values from 0 to 7, as said below
Outputs:
- covariance: float32 [4096, 4096], P('tensor', 'dp')
- cross_covariance: float32 [8, 4096], P(None, 'tensor')
Inputs may be any that keep to these rules, and one draw needn't show every extreme that they name: Every one of the 8 classes labels at least one token.
All inputs are finite; a program needn't handle non-finite values.
Results may differ from a plain program's by a relative error of at most 0.0003.
Values may be sent and summed in bfloat16 or wider, within the bound.
No kernel may reach another device: no remote copies, remote signals or barrier semaphores. Data moves between devices by JAX's collectives and lax.ppermute only.
A program may use at most 64 MiB of HBM per device.

v0:
```python
import jax
import jax.numpy as jnp
from jax import lax
from jax.sharding import PartitionSpec as P

D = 4096
CLASSES = 8


def body(activations, labels):
    tok_rows, slice_width = activations.shape
    token_total = tok_rows * lax.axis_size("dp")
    col_width = D // lax.axis_size("dp")
    classes = jnp.arange(CLASSES, dtype=jnp.int32)
    matches = labels[None, :] == classes[:, None]
    onehot = matches.astype(jnp.bfloat16)
    local_counts = jnp.sum(matches.astype(jnp.float32), axis=1)
    gathered = lax.all_gather(activations, "tensor", axis=1, tiled=True)
    gram_cols = lax.psum_scatter(
        lax.dot_general(
            gathered, activations, (((0,), (0,)), ((), ())), preferred_element_type=jnp.float32
        ),
        "dp",
        scatter_dimension=0,
        tiled=True,
    )
    slice_start = lax.axis_index("tensor") * slice_width
    wide_local = jnp.dot(onehot, gathered, preferred_element_type=jnp.float32)
    class_sums, class_counts = lax.psum((wide_local, local_counts), "dp")
    own_sums = lax.dynamic_slice_in_dim(class_sums, slice_start, slice_width, 1)
    overall_mean = jnp.sum(class_sums, axis=0) / token_total
    mean_rows = lax.dynamic_slice_in_dim(overall_mean, slice_start, slice_width, 0)
    mean_cols = lax.dynamic_slice_in_dim(
        overall_mean, lax.axis_index("dp") * col_width, col_width, 0
    )
    covariance = gram_cols.T / token_total - mean_rows[:, None] * mean_cols[None, :]
    cross_covariance = (own_sums - class_counts[:, None] * mean_rows[None, :]) / token_total
    return (covariance, cross_covariance)


def solution(mesh):
    in_specs = (P("dp", "tensor"), P("dp"))
    out_specs = (P("tensor", "dp"), P(None, "tensor"))
    return jax.shard_map(body, mesh=mesh, in_specs=in_specs, out_specs=out_specs, check_vma=False)
```

profile of v0, /device:TPU:2, one launch (start us, length us, event | category | flops | bytes accessed | tf_op | source)
XLA Modules:
  0.0 394.7 jit_solution(16058188507503878054)
XLA Ops:
  7.2 0.0 copy-start
  7.2 0.0 all-gather.2.cloned.1.call-start
  7.2 0.7 all-gather.2.cloned.1.call-update
  7.9 0.0 all-reduce.2.cloned.1.call-start
  8.0 135.1 %all-gather.2.cloned.1.call-done = bf16[1024,4096]{1,0:T(8,128)(2,1)} async-done(((bf16[1024,256]{1,0:T(8,128)(2,1)}), bf16[1024,4096]{1,0:T(8,128)(2,1)}) %all-gather.2.cloned.1.call-update) | async-done | bytes 8388624 | tf_op jit(solution)/shard_map/all_gather | solution.py:18
  143.1 5.2 %fusion = f32[8,4096]{1,0:T(8,128)} fusion(bf16[1024,4096]{1,0:T(8,128)(2,1)} %all-gather.2.cloned.1.call-done, s32[1024]{0:T(1024)} %param.3), kind=kOutput, calls=%fused_computation.3 | convolution fusion | flops 67117056 | bytes 8523776 | tf_op jit(solution)/shard_map/dot_general | solution.py:28
  148.3 0.0 all-reduce.2.cloned.1.call-update
  148.4 0.0 copy-start.1
  148.4 0.0 reduce-scatter.2.cloned.1.call-start
  148.4 0.0 copy-done
  148.4 7.8 %fusion.2 = f32[4096,256]{1,0:T(8,128)} fusion(bf16[1024,4096]{1,0:T(8,128)(2,1)} %all-gather.2.cloned.1.call-done, bf16[1024,256]{1,0:T(8,128)(2,1)S(1)} %copy-done), kind=kOutput, calls=%fused_computation.7 | convolution fusion | flops 2147483648 | bytes 13107200 | tf_op jit(solution)/shard_map/dot_general | solution.py:20
  156.2 0.0 reduce-scatter.2.cloned.1.call-update
  156.3 0.0 copy-done.1
  156.3 0.1 convert_reduce_fusion
  156.4 57.2 %psum.15 = f32[8]{0:T(128)S(1)} all-reduce(f32[8]{0:T(128)S(1)} %convert_reduce_fusion), channel_id=1, replica_groups=mesh['dp'=32,'tensor'=16] {'dp'}, use_global_device_ids=true, to_apply=%region_4.0 | all-reduce | flops 8 | bytes 64 | tf_op jit(solution)/shard_map/psum | solution.py:29
  213.6 62.8 %all-reduce.2.cloned.1.call-done = f32[8,4096]{1,0:T(8,128)} async-done(((f32[8,4096]{1,0:T(8,128)}), f32[8,4096]{1,0:T(8,128)}) %all-reduce.2.cloned.1.call-update) | async-done | bytes 131088 | tf_op jit(solution)/shard_map/psum | solution.py:29
  276.4 0.9 reduce_sum.18
  277.4 0.1 dynamic_slice.10
  277.5 0.1 dynamic_slice.9
  277.5 1.4 subtract_multiply_fusion
  278.9 107.5 %reduce-scatter.2.cloned.1.call-done = f32[128,256]{1,0:T(8,128)} async-done(((f32[4096,256]{1,0:T(8,128)}), f32[128,256]{1,0:T(8,128)}) %reduce-scatter.2.cloned.1.call-update) | async-done | bytes 131088 | tf_op jit(solution)/shard_map/reduce_scatter | solution.py:19
  386.4 1.0 bitcast_subtract_fusion
  387.4 0.8 copy.5
  (1 shorter events, 0.0 us)
Async XLA Ops:
  7.2 141.3 %copy-start = (bf16[1024,256]{1,0:T(8,128)(2,1)S(1)}, bf16[1024,256]{1,0:T(8,128)(2,1)}, u32[]{:S(2)}) copy-start(bf16[1024,256]{1,0:T(8,128)(2,1)} %param.2) | copy-start | bytes 1572868
  7.2 135.9 %all-gather.2.cloned.1.call-start = ((), (), s32[]{:S(2)}) async-start(), calls=%async_computation.1 | async-start | bytes 8912896 | tf_op jit(solution)/shard_map/all_gather | solution.py:18
  7.9 268.5 %all-reduce.2.cloned.1.call-start = ((), (), s32[]{:S(2)}) async-start(), calls=%async_computation.3 | async-start | bytes 262144 | tf_op jit(solution)/shard_map/psum | solution.py:29
  148.4 7.9 %copy-start.1 = (s32[1024]{0:T(1024)S(1)}, s32[1024]{0:T(1024)}, u32[]{:S(2)}) copy-start(s32[1024]{0:T(1024)} %param.3) | copy-start | bytes 12292
  148.4 238.0 %reduce-scatter.2.cloned.1.call-start = ((), (), s32[]{:S(2)}) async-start(), calls=%async_computation.2 | async-start | bytes 4325376 | tf_op jit(solution)/shard_map/reduce_scatter | solution.py:19
Sparse Core Ops, SparseCore 0:
  10.0 133.0 all-gather.1
  148.5 127.9 all-reduce.1
  281.0 105.3 reduce-scatter.1
where the time goes:
time: 395 us
  waiting for transfers between devices  306 us (77%)
  blocking collectives  57.2 us (14%)
  between operations  13.8 us (3%)
  matrix products  13.1 us (3%)
    all_gather x1, waiting for transfers between devices, body(): gathered = lax.all_gather(activations, 'tensor', axis=1, tiled=True)  135 us
    reduce_scatter x1, waiting for transfers between devices, body(): lax.psum_scatter(lax.dot_general(gathered, activations, (((0,), (0,)), ((...  107 us
    psum x1, waiting for transfers between devices, body(): class_sums, class_counts = lax.psum((wide_local, local_counts), 'dp')  62.8 us
    psum x1, blocking collectives, body(): class_sums, class_counts = lax.psum((wide_local, local_counts), 'dp')  57.2 us
  transfers between devices with their start and end apart: 3, of which 3 were waited for; matrix products, arithmetic and copies ran while one was open for 3% of the time, Pallas kernels for 0%

commit v1 on v0

--- a/solution.py
+++ b/solution.py
@@ -2,6 +2,7 @@
 import jax.numpy as jnp
 from jax import lax
 from jax.sharding import PartitionSpec as P
+from jax.lax import all_to_all, axis_size
 
 D = 4096
 CLASSES = 8
@@ -15,7 +16,16 @@
     matches = labels[None, :] == classes[:, None]
     onehot = matches.astype(jnp.bfloat16)
     local_counts = jnp.sum(matches.astype(jnp.float32), axis=1)
-    gathered = lax.all_gather(activations, "tensor", axis=1, tiled=True)
+
+    def flows_link(vec, dim_i=1):
+        rows = []
+        for _ in range(axis_size("tensor")):
+            rows.append(vec)
+        passed = jnp.stack(rows)
+        e_next = all_to_all(passed, split_axis=0, axis_name="tensor", concat_axis=0)
+        return jnp.concatenate(e_next, axis=dim_i)
+
+    gathered = flows_link(activations)
     gram_cols = lax.psum_scatter(
         lax.dot_general(
             gathered, activations, (((0,), (0,)), ((), ())), preferred_element_type=jnp.float32

time: 395 us -> 643 us (1.63)
  blocking collectives: 57.2 us -> 439 us
  waiting for transfers between devices: 306 us -> 169 us
    all_to_all x0 -> x1, blocking collectives: none -> 381 us  [flows_link(): e_next = all_to_all(passed, split_axis=0, axis_name='tensor', concat_axis=0)]
    all_gather x1 -> x0, waiting for transfers between devices: 135 us -> none  [body(): gathered = lax.all_gather(activations, 'tensor', axis=1, tiled=True)]
  transfers between devices with their start and end apart: 3 -> 2, of which waited for: 3 -> 2; matrix products, arithmetic and copies ran while one was open for 3% -> 2% of each run, Pallas kernels for 0% -> 0%
where the time goes in v1:
time: 643 us
  blocking collectives  439 us (68%)
  waiting for transfers between devices  169 us (26%)
  between operations  14.1 us (2%)
  matrix products  10.6 us (2%)
  local copies, waits for them, and re-layouts  6.48 us (1%)
    all_to_all x1, blocking collectives, flows_link(): e_next = all_to_all(passed, split_axis=0, axis_name='tensor', concat_axis=0)  381 us
    reduce_scatter x1, waiting for transfers between devices, body(): lax.psum_scatter(lax.dot_general(gathered, activations, (((0,), (0,)), ((...  107 us
    psum x1, waiting for transfers between devices, body(): class_sums, class_counts = lax.psum((wide_local, local_counts), 'dp')  61.7 us
    psum x1, blocking collectives, body(): class_sums, class_counts = lax.psum((wide_local, local_counts), 'dp')  57.6 us
  transfers between devices with their start and end apart: 2, of which 2 were waited for; matrix products, arithmetic and copies ran while one was open for 2% of the time, Pallas kernels for 0%

profile of v1, /device:TPU:2, one launch (start us, length us, event | category | flops | bytes accessed | tf_op | source)
XLA Modules:
  0.0 642.6 jit_solution(6151923051783647887)
XLA Ops:
  7.2 0.0 all-reduce.2.cloned.1.call-start
  7.2 1.2 copy.7
  8.5 1.1 stack.2
  9.6 0.0 copy-start.2
  9.6 381.2 %all_to_all.5 = bf16[16,1024,256]{1,2,0:T(8,128)(2,1)S(1)} all-to-all(bf16[16,1024,256]{1,2,0:T(8,128)(2,1)S(1)} %stack.2), channel_id=1, replica_groups=mesh['dp'=32,'tensor'=16] {'tensor'}, dimensions={0} | all-to-all | bytes 16777216 | tf_op jit(solution)/shard_map/all_to_all | solution.py:25
  390.7 0.0 copy-start
  390.7 0.0 copy-start.1
  390.7 3.2 copy-done
  394.0 0.0 copy-done.2
  394.0 2.9 fusion
  396.9 0.0 all-reduce.2.cloned.1.call-update
  396.9 0.0 reduce-scatter.2.cloned.1.call-start
  397.0 0.0 copy-done.1
  397.0 7.7 %fusion.2 = f32[4096,256]{1,0:T(8,128)} fusion(bf16[1024,4096]{0,1:T(8,128)(2,1)} %bitcast.9, bf16[1024,256]{1,0:T(8,128)(2,1)S(1)} %copy-done.1), kind=kOutput, calls=%fused_computation.7 | convolution fusion | flops 2147483648 | bytes 13107200 | tf_op jit(solution)/shard_map/dot_general | solution.py:30
  404.7 0.0 reduce-scatter.2.cloned.1.call-update
  404.7 0.1 convert_reduce_fusion
  404.8 57.6 %psum.15 = f32[8]{0:T(128)S(1)} all-reduce(f32[8]{0:T(128)S(1)} %convert_reduce_fusion), channel_id=1, replica_groups=mesh['dp'=32,'tensor'=16] {'dp'}, use_global_device_ids=true, to_apply=%region_4.0 | all-reduce | flops 8 | bytes 64 | tf_op jit(solution)/shard_map/psum | solution.py:39
  462.5 61.7 %all-reduce.2.cloned.1.call-done = f32[8,4096]{1,0:T(8,128)} async-done(((f32[8,4096]{1,0:T(8,128)}), f32[8,4096]{1,0:T(8,128)}) %all-reduce.2.cloned.1.call-update) | async-done | bytes 131088 | tf_op jit(solution)/shard_map/psum | solution.py:39
  524.1 0.9 reduce_sum.18
  525.1 0.1 dynamic_slice.10
  525.2 0.1 dynamic_slice.9
  525.2 1.4 subtract_multiply_fusion
  526.6 107.4 %reduce-scatter.2.cloned.1.call-done = f32[128,256]{1,0:T(8,128)} async-done(((f32[4096,256]{1,0:T(8,128)}), f32[128,256]{1,0:T(8,128)}) %reduce-scatter.2.cloned.1.call-update) | async-done | bytes 131088 | tf_op jit(solution)/shard_map/reduce_scatter | solution.py:29
  634.0 1.0 bitcast_subtract_fusion
  635.0 0.8 copy.8
  (1 shorter events, 0.0 us)
Async XLA Ops:
  7.2 517.0 %all-reduce.2.cloned.1.call-start = ((), (), s32[]{:S(2)}) async-start(), calls=%async_computation.3 | async-start | bytes 262144 | tf_op jit(solution)/shard_map/psum | solution.py:39
  9.6 384.4 %copy-start.2 = (s32[1024]{0:T(1024)S(1)}, s32[1024]{0:T(1024)}, u32[]{:S(2)}) copy-start(s32[1024]{0:T(1024)} %param.3) | copy-start | bytes 12292
  390.7 3.2 copy-start
  390.7 6.2 copy-start.1
  396.9 237.1 %reduce-scatter.2.cloned.1.call-start = ((), (), s32[]{:S(2)}) async-start(), calls=%async_computation.2 | async-start | bytes 4325376 | tf_op jit(solution)/shard_map/reduce_scatter | solution.py:29
Sparse Core Ops, SparseCore 0:
  397.0 127.0 all-reduce.1
  528.6 105.3 reduce-scatter.1
